TPU v7x, 32 devices: a whole 2x2x4 slice. The times are simulated.
32 devices in a mesh: rep: 4 (over y, core), shard: 8 (over z, x).
Axes of the slice: x: 2, y: 2, z: 4, core: 2. Of those that a mesh axis runs over, the one named last changes fastest.
Arguments:
- cell_features: bfloat16 [4, 4096, 1024], P('rep', 'shard'), may hold values from -10 to 10
- upstream: bfloat16 [4, 4096, 1024], P('rep', 'shard'), may hold values from -0.119628906 to 0.119628906
- qkv_weight: bfloat16 [4, 1024, 3072], P('rep', 'shard'), may hold values from -0.1875 to 0.1875
- out_weight: bfloat16 [4, 1024, 1024], P('rep', 'shard'), may hold values from -0.1875 to 0.1875
- momentum: float32 [4, 1024, 1024], P('rep', 'shard'), may hold values from -4 to 4
- key_tiles: int32 [4, 32, 6], P('rep'), may hold values from 0 to 31, as said below
- live_blocks: int32 [4, 32], P('rep'), may hold values from 1 to 6
- step_index: int32 [], replicated, may hold values from 0 to 999
Outputs:
- layer_out: bfloat16 [4, 4096, 1024], P('rep', 'shard')
- new_weight: bfloat16 [4, 1024, 1024], P('rep', 'shard')
- new_momentum: float32 [4, 1024, 1024], P('rep', 'shard')
Inputs may be any that keep to these rules, and one draw needn't show every extreme that they name: `key_tiles`: every entry names a tile of its group. Of the 24 entries of device d's 4 query tiles (tiles d*4 to (d+1)*4 - 1), exactly 12 name tiles of device d itself (tile // 4 == d); of the others at most 2 name tiles of any one other device, and in every draw some device is named exactly 2 times.
All inputs are finite; a program needn't handle non-finite values.
Results may differ from a plain program's by a relative error of at most 0.025.
Values may be sent and summed in bfloat16 or wider, within the bound.
No kernel may reach another device: no remote copies, remote signals or barrier semaphores. Data moves between devices by JAX's collectives and lax.ppermute only.
A program may use at most 128 MiB of HBM per device.

v0:
```python
import functools
import jax
import jax.numpy as jnp
from jax import lax
from jax.sharding import PartitionSpec as P

HEADS = 16
HEAD_DIM = 64
TILE = 128
KB = 6
momentum_beta = 0.9


def shortened(value):

    def short(part):
        return part.astype(jnp.bfloat16) if part.dtype == jnp.float32 else part

    return jax.tree.map(short, value)


def partner(value, axis, bit):
    return lax.ppermute(value, axis, [(i, i ^ 1 << bit) for i in range(lax.axis_size(axis))])


def add_rows(source, shard_rows):
    return jnp.dot(source, shard_rows, preferred_element_type=jnp.float32)


def attend_tile(local_table, arrived_table, element):
    query_tile, is_remote, local_index, arrive_index, live_count = element
    model_width = query_tile.shape[1]
    from_local = local_table[local_index]
    from_remote = arrived_table[arrive_index]
    key_value = jnp.where(is_remote[:, None, None], from_remote, from_local).reshape(
        KB * TILE, 2 * model_width
    )
    query_split = query_tile.reshape(TILE, HEADS, HEAD_DIM)
    keys_split = key_value[:, :model_width].reshape(KB * TILE, HEADS, HEAD_DIM)
    values_split = key_value[:, model_width:].reshape(KB * TILE, HEADS, HEAD_DIM)
    scores = jnp.einsum(
        "qhd,khd->hqk", query_split, keys_split, preferred_element_type=jnp.float32
    ) * HEAD_DIM ** (-0.5)
    usable = jnp.arange(KB * TILE, dtype=jnp.int32) // TILE < live_count
    scores = jnp.where(usable[None, None, :], scores, jnp.float32(-1e30))
    row_max = jnp.max(scores, axis=2, keepdims=True)
    exponent = jnp.exp(scores - row_max)
    probabilities = (exponent / jnp.sum(exponent, axis=2, keepdims=True)).astype(jnp.bfloat16)
    mixture = jnp.einsum(
        "hqk,khd->qhd", probabilities, values_split, preferred_element_type=jnp.float32
    )
    return mixture.reshape(TILE, model_width).astype(jnp.bfloat16)


def swap_with(bit_number, stacked_pair):
    return jax.tree.map(
        lambda part, own: part.astype(own.dtype),
        partner(shortened(stacked_pair), "rep", bit_number),
        stacked_pair,
    )


def body(
    cell_features, upstream, qkv_weight, out_weight, momentum, key_tiles, live_blocks, step_index
):
    features = cell_features[0]
    row_count, model_width = features.shape
    tile_count = row_count // TILE
    shard_count = lax.axis_size("shard")
    my_index = lax.axis_index("shard")
    slot_count = tile_count * KB
    remote_count = slot_count - slot_count // 2
    capacity = (remote_count + shard_count - 2) // (shard_count - 1)
    requests = key_tiles[0].reshape(shard_count, slot_count)
    owners = requests // tile_count
    local_tile = requests % tile_count
    requester = jnp.arange(shard_count, dtype=jnp.int32)[:, None]
    elsewhere = owners != requester
    positions = jnp.arange(slot_count, dtype=jnp.int32)
    earlier = positions[None, :] < positions[:, None]
    same_owner = owners[:, :, None] == owners[:, None, :]
    owner_rank = jnp.sum((same_owner & earlier[None]).astype(jnp.int32), axis=2)
    owned = (owners == my_index) & elsewhere
    slot_ids = jnp.arange(capacity, dtype=jnp.int32)
    chosen = owned[:, :, None] & (owner_rank[:, :, None] == slot_ids[None, None, :])
    send_index = jnp.sum(chosen.astype(jnp.int32) * local_tile[:, :, None], axis=1).reshape(-1)
    send_valid = jnp.any(chosen, axis=1).reshape(-1)
    my_owners = lax.dynamic_index_in_dim(owners, my_index, 0, keepdims=False)
    my_ranks = lax.dynamic_index_in_dim(owner_rank, my_index, 0, keepdims=False)
    my_local = lax.dynamic_index_in_dim(local_tile, my_index, 0, keepdims=False)
    my_remote = my_owners != my_index
    arrive_index = jnp.where(my_remote, my_owners * capacity + my_ranks, 0)
    local_index = jnp.where(my_remote, 0, my_local)
    projected = add_rows(
        features, lax.all_gather(qkv_weight[0], "shard", axis=0, tiled=True)
    ).astype(jnp.bfloat16)
    picked = projected[:, model_width:].reshape(tile_count, TILE, 2 * model_width)[send_index]
    sent = jnp.where(send_valid[:, None, None], picked, jnp.zeros_like(picked)).reshape(
        shard_count, capacity, TILE, 2 * model_width
    )
    arrived = lax.all_to_all(sent, "shard", split_axis=0, concat_axis=0, tiled=True)
    arrived_table = arrived.reshape(shard_count * capacity, TILE, 2 * model_width)
    query = projected[:, :model_width].reshape(tile_count, TILE, model_width)
    local_table = projected[:, model_width:].reshape(tile_count, TILE, 2 * model_width)
    live_mine = lax.dynamic_slice_in_dim(live_blocks[0], my_index * tile_count, tile_count, 0)
    per_tile = functools.partial(attend_tile, local_table, arrived_table)
    elements = (
        query,
        my_remote.reshape(tile_count, KB),
        local_index.reshape(tile_count, KB),
        arrive_index.reshape(tile_count, KB),
        live_mine,
    )
    attended = lax.map(per_tile, elements).reshape(row_count, model_width)
    product = add_rows(attended, lax.all_gather(out_weight[0], "shard", axis=0, tiled=True))
    layer_out = (features.astype(jnp.float32) + product).astype(jnp.bfloat16)
    gradient = lax.psum_scatter(
        lax.dot_general(
            attended, upstream[0], (((0,), (0,)), ((), ())), preferred_element_type=jnp.float32
        ).astype(jnp.bfloat16),
        "shard",
        scatter_dimension=0,
        tiled=True,
    ).astype(jnp.float32)
    learn_rate = jnp.float32(50.0) / (jnp.float32(500.0) + step_index.astype(jnp.float32))
    velocity = momentum_beta * momentum[0] + gradient
    stepped = (out_weight[0].astype(jnp.float32) - learn_rate * velocity).astype(jnp.bfloat16)
    stacked_pair = jnp.stack([stepped.astype(jnp.float32), velocity])
    bit_count = lax.axis_size("rep").bit_length() - 1
    branches = [functools.partial(swap_with, bit_number) for bit_number in range(bit_count)]
    bit_choice = step_index % bit_count
    partner_pair = lax.switch(bit_choice, branches, stacked_pair)
    averaged = 0.5 * (stacked_pair + partner_pair)
    new_weight = averaged[0].astype(jnp.bfloat16)
    new_momentum = averaged[1]
    return (layer_out[None], new_weight[None], new_momentum[None])


def solution(mesh):
    placed = (
        P("rep", "shard", None),
        P("rep", "shard", None),
        P("rep", "shard", None),
        P("rep", "shard", None),
        P("rep", "shard", None),
        P("rep", None, None),
        P("rep", None),
        P(),
    )
    return jax.shard_map(
        body,
        mesh=mesh,
        in_specs=placed,
        out_specs=(P("rep", "shard", None), P("rep", "shard", None), P("rep", "shard", None)),
        check_vma=False,
    )
```

profile of v0, /device:TPU:0, one launch (start us, length us, event | category | flops | bytes accessed | tf_op | source)
XLA Modules:
  0.0 585.2 jit_solution(10328500597849223528)
XLA Ops:
  7.9 0.8 copy.21
  9.7 101.9 %all-gather.5.cloned.1.call-done = bf16[1,1024,3072]{2,1,0:T(8,128)(2,1)} async-done(((bf16[1,128,3072]{2,1,0:T(8,128)(2,1)}), bf16[1,1024,3072]{2,1,0:T(8,128)(2,1)}) %all-gather.5.cloned.1.call-update) | async-done | bytes 6291472 | tf_op jit(solution)/shard_map/all_gather | solution.py:95
  111.6 6.5 %fusion.21 = bf16[512,3072]{1,0:T(8,128)(2,1)S(1)} fusion(bf16[1,1024,3072]{2,1,0:T(8,128)(2,1)} %all-gather.5.cloned.1.call-done, bf16[1,512,1024]{2,1,0:T(8,128)(2,1)} %param.12), kind=kOutput, calls=%fused_computation.42 | convolution fusion | flops 3222798336 | bytes 10485760 | tf_op jit(solution)/shard_map/dot_general | solution.py:27
  118.2 1.6 copy-done.1
  120.0 4.6 gather_fusion.2
  124.7 7.2 %broadcast_select_fusion.1 = bf16[8,2,128,2048]{3,2,1,0:T(8,128)(2,1)} fusion(bf16[8,2,128,2048]{3,2,1,0:T(8,128)(2,1)} %bitcast.120, pred[8,2]{1,0:T(8,128)(4,1)S(1)} %copy.22), kind=kLoop, calls=%fused_computation.39 | loop fusion | flops 4194304 | bytes 16777232 | tf_op jit(solution)/shard_map/jit(_where)/select_n | solution.py:98
  131.9 5.1 all-to-all-start
  138.3 2.3 slice.39
  140.6 203.7 %all-to-all-done = bf16[8,2,128,2048]{3,2,1,0:T(8,128)(2,1)} async-done(((bf16[8,2,128,2048]{3,2,1,0:T(8,128)(2,1)}), bf16[8,2,128,2048]{3,2,1,0:T(8,128)(2,1)}, u32[]{:S(2)}, u32[]{:S(2)}) %all-to-all-start) | async-done | bytes 8388640 | tf_op jit(solution)/shard_map/all_to_all | solution.py:101
  344.3 157.9 %while.12 = (s32[]{:T(128)}, bf16[4,128,1024]{2,1,0:T(8,128)(2,1)}, pred[4,6]{1,0:T(4,128)(4,1)S(1)}, s32[4,6]{1,0:T(4,128)S(1)}, bf16[16,128,2048]{2,1,0:T(8,12...) while((s32[]{:T(128)}, bf16[4,128,1024]{2,1,0:T(8,128)(2,1)}, ...), condition=%wide.region_6.7_spmd, body=%wide.region_3.6_spmd.sunk | while | flops 413804064 | bytes 59273044 | solution.py:114
  344.3 6.0 %gather_fusion = bf16[6,128,2048]{2,1,0:T(8,128)(2,1)} fusion(bf16[16,128,2048]{2,1,0:T(8,128)(2,1)} %get-tuple-element.279, s32[1024]{0:T(1024)S(1)} %pad_clamp_fusion.5), kind=kCustom, calls=%fused_computation.clone.1 | custom fusion | bytes 6291480 | tf_op jit(solution)/shard_map/while/body/eval_jaxpr/gather | solution.py:34
  350.3 4.7 copy.33
  355.0 2.5 gather_fusion.1
  357.4 4.6 copy.34
  362.2 3.2 broadcast_select_fusion.5
  365.4 1.8 fusion.68
  367.2 1.0 constant_dynamic-slice_fusion.8
  368.1 0.8 copy.35
  370.3 6.4 %fusion.70 = (f32[16,128]{1,0:T(8,128)S(1)}, f32[16,128,768]{2,1,0:T(8,128)}) fusion(pred[768]{0:T(1024)(128)(4,1)S(1)} %fusion.69, bf16[128,16,64]{0,2,1:T(8,128)(2,1)} %bitcast.121, bf16[768,16,64]{0,2,1:T(8,128)(2,1)} %bitcast.119), kind=kOutput, calls=%fused_computation.90.clone.1 | convolution fusion | flops 207618816 | bytes 8135424 | tf_op jit(solution)/shard_map/while/body/eval_jaxpr/sub | solution.py:47
  376.7 5.3 fusion.71
  381.9 1.1 copy.36
  383.8 6.0 %gather_fusion = bf16[6,128,2048]{2,1,0:T(8,128)(2,1)} fusion(bf16[16,128,2048]{2,1,0:T(8,128)(2,1)} %get-tuple-element.279, s32[1024]{0:T(1024)S(1)} %pad_clamp_fusion.5), kind=kCustom, calls=%fused_computation.clone.1 | custom fusion | bytes 6291480 | tf_op jit(solution)/shard_map/while/body/eval_jaxpr/gather | solution.py:34
  389.8 4.7 copy.33
  394.4 2.5 gather_fusion.1
  396.9 4.6 copy.34
  401.6 3.2 broadcast_select_fusion.5
  404.8 1.8 fusion.68
  406.6 1.0 constant_dynamic-slice_fusion.8
  407.6 0.8 copy.35
  409.7 6.4 %fusion.70 = (f32[16,128]{1,0:T(8,128)S(1)}, f32[16,128,768]{2,1,0:T(8,128)}) fusion(pred[768]{0:T(1024)(128)(4,1)S(1)} %fusion.69, bf16[128,16,64]{0,2,1:T(8,128)(2,1)} %bitcast.121, bf16[768,16,64]{0,2,1:T(8,128)(2,1)} %bitcast.119), kind=kOutput, calls=%fused_computation.90.clone.1 | convolution fusion | flops 207618816 | bytes 8135424 | tf_op jit(solution)/shard_map/while/body/eval_jaxpr/sub | solution.py:47
  416.1 5.3 fusion.71
  421.4 1.1 copy.36
  422.5 0.7 constant_dynamic-update-slice_fusion.2
  423.3 6.0 %gather_fusion = bf16[6,128,2048]{2,1,0:T(8,128)(2,1)} fusion(bf16[16,128,2048]{2,1,0:T(8,128)(2,1)} %get-tuple-element.279, s32[1024]{0:T(1024)S(1)} %pad_clamp_fusion.5), kind=kCustom, calls=%fused_computation.clone.1 | custom fusion | bytes 6291480 | tf_op jit(solution)/shard_map/while/body/eval_jaxpr/gather | solution.py:34
  429.2 4.7 copy.33
  433.9 2.5 gather_fusion.1
  436.4 4.6 copy.34
  441.1 3.2 broadcast_select_fusion.5
  444.3 1.8 fusion.68
  446.1 1.0 constant_dynamic-slice_fusion.8
  447.1 0.8 copy.35
  449.2 6.4 %fusion.70 = (f32[16,128]{1,0:T(8,128)S(1)}, f32[16,128,768]{2,1,0:T(8,128)}) fusion(pred[768]{0:T(1024)(128)(4,1)S(1)} %fusion.69, bf16[128,16,64]{0,2,1:T(8,128)(2,1)} %bitcast.121, bf16[768,16,64]{0,2,1:T(8,128)(2,1)} %bitcast.119), kind=kOutput, calls=%fused_computation.90.clone.1 | convolution fusion | flops 207618816 | bytes 8135424 | tf_op jit(solution)/shard_map/while/body/eval_jaxpr/sub | solution.py:47
  455.6 5.3 fusion.71
  460.9 1.1 copy.36
  462.0 0.7 constant_dynamic-update-slice_fusion.2
  462.8 6.0 %gather_fusion = bf16[6,128,2048]{2,1,0:T(8,128)(2,1)} fusion(bf16[16,128,2048]{2,1,0:T(8,128)(2,1)} %get-tuple-element.279, s32[1024]{0:T(1024)S(1)} %pad_clamp_fusion.5), kind=kCustom, calls=%fused_computation.clone.1 | custom fusion | bytes 6291480 | tf_op jit(solution)/shard_map/while/body/eval_jaxpr/gather | solution.py:34
  468.7 4.7 copy.33
  473.4 2.5 gather_fusion.1
  475.9 4.6 copy.34
  480.6 3.2 broadcast_select_fusion.5
  483.8 1.8 fusion.68
  485.6 1.0 constant_dynamic-slice_fusion.8
  486.6 0.8 copy.35
  488.7 6.4 %fusion.70 = (f32[16,128]{1,0:T(8,128)S(1)}, f32[16,128,768]{2,1,0:T(8,128)}) fusion(pred[768]{0:T(1024)(128)(4,1)S(1)} %fusion.69, bf16[128,16,64]{0,2,1:T(8,128)(2,1)} %bitcast.121, bf16[768,16,64]{0,2,1:T(8,128)(2,1)} %bitcast.119), kind=kOutput, calls=%fused_computation.90.clone.1 | convolution fusion | flops 207618816 | bytes 8135424 | tf_op jit(solution)/shard_map/while/body/eval_jaxpr/sub | solution.py:47
  495.1 5.3 fusion.71
  500.4 1.1 copy.36
  502.2 3.9 convolution_convert_fusion
  506.9 4.2 fusion.28
  511.1 62.4 %reduce-scatter.2.cloned.1.call-done = bf16[128,1024]{1,0:T(8,128)(2,1)} async-done(((bf16[1024,1024]{1,0:T(8,128)(2,1)}), bf16[128,1024]{1,0:T(8,128)(2,1)}) %reduce-scatter.2.cloned.1.call-update) | async-done | bytes 262160 | tf_op jit(solution)/shard_map/reduce_scatter | solution.py:117
  573.6 1.1 fusion.36
  574.7 2.1 conditional.4
  574.8 1.9 collective-permute-done
  577.1 0.8 slice.41
  577.9 0.7 slice.43
  (73 shorter events, 10.7 us)
Async XLA Ops:
  7.2 495.0 %copy-start = (bf16[1,512,1024]{2,1,0:T(8,128)(2,1)S(1)}, bf16[1,512,1024]{2,1,0:T(8,128)(2,1)}, u32[]{:S(2)}) copy-start(bf16[1,512,1024]{2,1,0:T(8,128)(2,1)} %param.13) | copy-start | bytes 3145732
  7.2 104.4 %all-gather.5.cloned.1.call-start = ((), (), s32[]{:S(2)}) async-start(), calls=%async_computation.3 | async-start | bytes 7077888 | tf_op jit(solution)/shard_map/all_gather | solution.py:95
  118.2 1.7 copy-start.1
  131.9 6.4 %copy-start.5 = (s32[1,32]{1,0:T(1,128)S(1)}, s32[1,32]{1,0:T(1,128)}, u32[]{:S(2)}) copy-start(s32[1,32]{1,0:T(1,128)} %param.18) | copy-start | bytes 388
  131.9 212.4 %all-to-all-start = ((bf16[8,2,128,2048]{3,2,1,0:T(8,128)(2,1)}), bf16[8,2,128,2048]{3,2,1,0:T(8,128)(2,1)}, u32[]{:S(2)}, u32[]{:S(2)}) async-start(bf16[8,2,128,2048]{3,2,1,0:T(8,128)(2,1)} %broadcast_select_fusion.1), calls=%async_computation | async-start | bytes 16777216 | tf_op jit(solution)/shard_map/all_to_all | solution.py:101
  136.9 370.0 %all-gather.7.cloned.1.call-start = ((), (), s32[]{:S(2)}) async-start(), calls=%async_computation.4 | async-start | bytes 2359296 | tf_op jit(solution)/shard_map/all_gather | solution.py:115
  137.7 435.9 %reduce-scatter.2.cloned.1.call-start = ((), (), s32[]{:S(2)}) async-start(), calls=%async_computation.2 | async-start | bytes 2359296 | tf_op jit(solution)/shard_map/reduce_scatter | solution.py:117
  502.2 4.7 copy-start.4
  506.9 66.7 %copy-start.2 = (bf16[1,128,1024]{2,1,0:T(8,128)(2,1)S(1)}, bf16[1,128,1024]{2,1,0:T(8,128)(2,1)}, u32[]{:S(2)}) copy-start(bf16[1,128,1024]{2,1,0:T(8,128)(2,1)} %param.15) | copy-start | bytes 786436
  506.9 66.7 %copy-start.3 = (f32[1,128,1024]{2,1,0:T(8,128)S(1)}, f32[1,128,1024]{2,1,0:T(8,128)}, u32[]{:S(2)}) copy-start(f32[1,128,1024]{2,1,0:T(8,128)} %param.16) | copy-start | bytes 1572868
  574.8 2.0 collective-permute-start
Sparse Core Ops, SparseCore 0:
  10.2 101.3 all-gather.4
  139.9 169.2 all-gather.6
  506.3 67.2 reduce-scatter.1
where the time goes:
time: 587 us; the launch traced here: 585 us
  waiting for transfers between devices  371 us (63%)
  local copies, waits for them, and re-layouts  108 us (18%)
  matrix products  61.4 us (10%)
  other arithmetic  24.6 us (4%)
  between operations  14.6 us (2%)
    all_to_all x1, waiting for transfers between devices, body(): lax.all_to_all(sent, 'shard', split_axis=0, concat_axis=0, tiled=True)  204 us
    all_gather x1, waiting for transfers between devices, body(): lax.all_gather(qkv_weight[0], 'shard', axis=0, tiled=True)  102 us
    reduce_scatter x1, waiting for transfers between devices, body(): lax.psum_scatter(lax.dot_general(attended, upstream[0], (((0,), (0,)), ((...  62.4 us
    gather x8, local copies, waits for them, and re-layouts, attend_tile(): from_remote = arrived_table[arrive_index]  42.6 us
    gather x8, local copies, waits for them, and re-layouts, attend_tile(): from_local = local_table[local_index]  28.5 us
    sub x4, matrix products, attend_tile(): exponent = jnp.exp(scores - row_max)  25.6 us
    dot_general x4, matrix products, attend_tile(): jnp.einsum('hqk,khd->qhd', probabilities, values_split, preferred_element...  21.1 us
    select_n x4, other arithmetic, attend_tile(): jnp.where(is_remote[:, None, None], from_remote, from_local)  12.7 us
  transfers between devices with their start and end apart: 5, of which 4 were waited for; matrix products, arithmetic and copies ran while one was open for 29% of the time, Pallas kernels for 0%

commit v1 on v0

--- a/solution.py
+++ b/solution.py
@@ -9,6 +9,19 @@
 TILE = 128
 KB = 6
 momentum_beta = 0.9
+
+
+def collect(x, axis, dim):
+    size, index, span = (lax.axis_size(axis), lax.axis_index(axis), x.shape[dim])
+    right = [(i, (i + 1) % size) for i in range(size)]
+    out = jnp.zeros((*x.shape[:dim], size * span, *x.shape[dim + 1 :]), x.dtype)
+    held = x
+    for step in range(size):
+        holder = (index - step) % size
+        out = lax.dynamic_update_slice_in_dim(out, held, holder * span, axis=dim)
+        if step < size - 1:
+            held = lax.ppermute(held, axis, right)
+    return out
 
 
 def shortened(value):
@@ -91,9 +104,7 @@
     my_remote = my_owners != my_index
     arrive_index = jnp.where(my_remote, my_owners * capacity + my_ranks, 0)
     local_index = jnp.where(my_remote, 0, my_local)
-    projected = add_rows(
-        features, lax.all_gather(qkv_weight[0], "shard", axis=0, tiled=True)
-    ).astype(jnp.bfloat16)
+    projected = add_rows(features, collect(qkv_weight[0], "shard", 0)).astype(jnp.bfloat16)
     picked = projected[:, model_width:].reshape(tile_count, TILE, 2 * model_width)[send_index]
     sent = jnp.where(send_valid[:, None, None], picked, jnp.zeros_like(picked)).reshape(
         shard_count, capacity, TILE, 2 * model_width

time: 587 us -> 615 us (1.048)
  waiting for transfers between devices: 371 us -> 395 us
    ppermute x0 -> x7, waiting for transfers between devices: none -> 132 us  [collect(): held = lax.ppermute(held, axis, right)]
    all_gather x1 -> x0, waiting for transfers between devices: 102 us -> none  [body(): lax.all_gather(qkv_weight[0], 'shard', axis=0, tiled=True)]
  transfers between devices with their start and end apart: 5 -> 11, of which waited for: 4 -> 10; matrix products, arithmetic and copies ran while one was open for 29% -> 28% of each run, Pallas kernels for 0% -> 0%
where the time goes in v1:
time: 615 us; the launch traced here: 613 us
  waiting for transfers between devices  395 us (64%)
  local copies, waits for them, and re-layouts  111 us (18%)
  matrix products  58.4 us (9%)
  other arithmetic  24.7 us (4%)
  between operations  15.1 us (2%)
  starting transfers between devices  8.43 us (1%)
    all_to_all x1, waiting for transfers between devices, body(): lax.all_to_all(sent, 'shard', split_axis=0, concat_axis=0, tiled=True)  199 us
    ppermute x7, waiting for transfers between devices, collect(): held = lax.ppermute(held, axis, right)  132 us
    reduce_scatter x1, waiting for transfers between devices, body(): lax.psum_scatter(lax.dot_general(attended, upstream[0], (((0,), (0,)), ((...  61.7 us
    gather x8, local copies, waits for them, and re-layouts, attend_tile(): from_remote = arrived_table[arrive_index]  42.7 us
    gather x8, local copies, waits for them, and re-layouts, attend_tile(): from_local = local_table[local_index]  28.5 us
    sub x4, matrix products, attend_tile(): exponent = jnp.exp(scores - row_max)  25.5 us
    dot_general x4, matrix products, attend_tile(): jnp.einsum('hqk,khd->qhd', probabilities, values_split, preferred_element...  21.1 us
    select_n x4, other arithmetic, attend_tile(): jnp.where(is_remote[:, None, None], from_remote, from_local)  12.7 us
  transfers between devices with their start and end apart: 11, of which 10 were waited for; matrix products, arithmetic and copies ran while one was open for 28% of the time, Pallas kernels for 0%

profile of v1, /device:TPU:0, one launch (start us, length us, event | category | flops | bytes accessed | tf_op | source)
XLA Modules:
  0.0 613.1 jit_solution(6889668086939195370)
XLA Ops:
  7.2 3.0 collective-permute-start.2
  10.2 20.8 %collective-permute-done.2 = bf16[128,3072]{1,0:T(8,128)(2,1)S(1)} collective-permute-done((bf16[128,3072]{1,0:T(8,128)(2,1)}, bf16[128,3072]{1,0:T(8,128)(2,1)S(1)}, u32[]{:S(2)}, u32[]{:S(2)}) %collective-permute-start.2) | collective-permute-done | bytes 786464 | tf_op jit(solution)/shard_map/ppermute | solution.py:23
  31.0 21.4 %collective-permute-done.3 = bf16[128,3072]{1,0:T(8,128)(2,1)S(1)} collective-permute-done((bf16[128,3072]{1,0:T(8,128)(2,1)S(1)}, bf16[128,3072]{1,0:T(8,128)(2,1)S(1)}, u32[]{:S(2)}, u32[]{:S(2)}) %collective-permute-start.3) | collective-permute-done | bytes 786464 | tf_op jit(solution)/shard_map/ppermute | solution.py:23
  53.3 19.8 %collective-permute-done.4 = bf16[128,3072]{1,0:T(8,128)(2,1)} collective-permute-done((bf16[128,3072]{1,0:T(8,128)(2,1)S(1)}, bf16[128,3072]{1,0:T(8,128)(2,1)}, u32[]{:S(2)}, u32[]{:S(2)}) %collective-permute-start.4) | collective-permute-done | bytes 786464 | tf_op jit(solution)/shard_map/ppermute | solution.py:23
  73.9 19.1 %collective-permute-done.5 = bf16[128,3072]{1,0:T(8,128)(2,1)} collective-permute-done((bf16[128,3072]{1,0:T(8,128)(2,1)}, bf16[128,3072]{1,0:T(8,128)(2,1)}, u32[]{:S(2)}, u32[]{:S(2)}) %collective-permute-start.5) | collective-permute-done | bytes 786464 | tf_op jit(solution)/shard_map/ppermute | solution.py:23
  94.0 18.1 %collective-permute-done.6 = bf16[128,3072]{1,0:T(8,128)(2,1)S(1)} collective-permute-done((bf16[128,3072]{1,0:T(8,128)(2,1)}, bf16[128,3072]{1,0:T(8,128)(2,1)S(1)}, u32[]{:S(2)}, u32[]{:S(2)}) %collective-permute-start.6) | collective-permute-done | bytes 786464 | tf_op jit(solution)/shard_map/ppermute | solution.py:23
  112.3 1.2 constant_dynamic-update-slice_fusion.5
  113.5 16.6 %collective-permute-done.7 = bf16[128,3072]{1,0:T(8,128)(2,1)S(1)} collective-permute-done((bf16[128,3072]{1,0:T(8,128)(2,1)S(1)}, bf16[128,3072]{1,0:T(8,128)(2,1)S(1)}, u32[]{:S(2)}, u32[]{:S(2)}) %collective-permute-start.7) | collective-permute-done | bytes 786464 | tf_op jit(solution)/shard_map/ppermute | solution.py:23
  130.1 1.2 constant_dynamic-update-slice_fusion.4
  131.5 15.8 %collective-permute-done.8 = bf16[128,3072]{1,0:T(8,128)(2,1)S(1)} collective-permute-done((bf16[128,3072]{1,0:T(8,128)(2,1)S(1)}, bf16[128,3072]{1,0:T(8,128)(2,1)S(1)}, u32[]{:S(2)}, u32[]{:S(2)}) %collective-permute-start.8) | collective-permute-done | bytes 786464 | tf_op jit(solution)/shard_map/ppermute | solution.py:23
  147.3 3.7 fusion.19
  151.0 1.6 copy-done.1
  152.8 4.7 gather_fusion.2
  157.5 7.2 %broadcast_select_fusion.1 = bf16[8,2,128,2048]{3,2,1,0:T(8,128)(2,1)} fusion(bf16[8,2,128,2048]{3,2,1,0:T(8,128)(2,1)} %bitcast.120, pred[8,2]{1,0:T(8,128)(4,1)S(1)} %copy.22), kind=kLoop, calls=%fused_computation.39 | loop fusion | flops 4194304 | bytes 16777232 | tf_op jit(solution)/shard_map/jit(_where)/select_n | solution.py:109
  164.7 5.1 all-to-all-start
  171.1 2.3 slice.39
  173.4 199.3 %all-to-all-done = bf16[8,2,128,2048]{3,2,1,0:T(8,128)(2,1)} async-done(((bf16[8,2,128,2048]{3,2,1,0:T(8,128)(2,1)}), bf16[8,2,128,2048]{3,2,1,0:T(8,128)(2,1)}, u32[]{:S(2)}, u32[]{:S(2)}) %all-to-all-start) | async-done | bytes 8388640 | tf_op jit(solution)/shard_map/all_to_all | solution.py:112
  372.7 157.8 %while.12 = (s32[]{:T(128)}, bf16[4,128,1024]{2,1,0:T(8,128)(2,1)}, pred[4,6]{1,0:T(4,128)(4,1)S(1)}, s32[4,6]{1,0:T(4,128)S(1)}, bf16[16,128,2048]{2,1,0:T(8,12...) while((s32[]{:T(128)}, bf16[4,128,1024]{2,1,0:T(8,128)(2,1)}, ...), condition=%wide.region_6.7_spmd, body=%wide.region_3.6_spmd.sunk | while | flops 413804064 | bytes 59273044 | solution.py:125
  372.8 6.0 gather_fusion
  378.7 4.7 copy.33
  383.4 2.5 gather_fusion.1
  385.9 4.6 copy.34
  390.6 3.2 broadcast_select_fusion.5
  393.8 1.8 fusion.65
  395.7 1.0 constant_dynamic-slice_fusion.8
  398.7 6.4 %fusion.67 = (f32[16,128]{1,0:T(8,128)S(1)}, f32[16,128,768]{2,1,0:T(8,128)}) fusion(pred[768]{0:T(1024)(128)(4,1)S(1)} %fusion.66, bf16[128,16,64]{0,2,1:T(8,128)(2,1)} %bitcast.121, bf16[768,16,64]{0,2,1:T(8,128)(2,1)} %bitcast.119), kind=kOutput, calls=%fused_computation.97.clone.1 | convolution fusion | flops 207618816 | bytes 8135424 | tf_op jit(solution)/shard_map/while/body/eval_jaxpr/sub | solution.py:60
  405.1 5.3 fusion.68
  410.4 1.1 copy.36
  412.2 6.0 gather_fusion
  418.2 4.7 copy.33
  422.9 2.5 gather_fusion.1
  425.4 4.6 copy.34
  430.1 3.2 broadcast_select_fusion.5
  433.3 1.8 fusion.65
  435.1 1.0 constant_dynamic-slice_fusion.8
  438.2 6.4 %fusion.67 = (f32[16,128]{1,0:T(8,128)S(1)}, f32[16,128,768]{2,1,0:T(8,128)}) fusion(pred[768]{0:T(1024)(128)(4,1)S(1)} %fusion.66, bf16[128,16,64]{0,2,1:T(8,128)(2,1)} %bitcast.121, bf16[768,16,64]{0,2,1:T(8,128)(2,1)} %bitcast.119), kind=kOutput, calls=%fused_computation.97.clone.1 | convolution fusion | flops 207618816 | bytes 8135424 | tf_op jit(solution)/shard_map/while/body/eval_jaxpr/sub | solution.py:60
  444.5 5.3 fusion.68
  449.8 1.1 copy.36
  451.7 6.0 gather_fusion
  457.6 4.7 copy.33
  462.3 2.5 gather_fusion.1
  464.8 4.6 copy.34
  469.5 3.2 broadcast_select_fusion.5
  472.7 1.8 fusion.65
  474.6 1.0 constant_dynamic-slice_fusion.8
  477.6 6.4 %fusion.67 = (f32[16,128]{1,0:T(8,128)S(1)}, f32[16,128,768]{2,1,0:T(8,128)}) fusion(pred[768]{0:T(1024)(128)(4,1)S(1)} %fusion.66, bf16[128,16,64]{0,2,1:T(8,128)(2,1)} %bitcast.121, bf16[768,16,64]{0,2,1:T(8,128)(2,1)} %bitcast.119), kind=kOutput, calls=%fused_computation.97.clone.1 | convolution fusion | flops 207618816 | bytes 8135424 | tf_op jit(solution)/shard_map/while/body/eval_jaxpr/sub | solution.py:60
  484.0 5.3 fusion.68
  489.3 1.1 copy.36
  491.1 6.0 gather_fusion
  497.1 4.7 copy.33
  501.8 2.5 gather_fusion.1
  504.3 4.6 copy.34
  509.0 3.2 broadcast_select_fusion.5
  512.2 1.8 fusion.65
  514.0 1.0 constant_dynamic-slice_fusion.8
  517.0 6.4 %fusion.67 = (f32[16,128]{1,0:T(8,128)S(1)}, f32[16,128,768]{2,1,0:T(8,128)}) fusion(pred[768]{0:T(1024)(128)(4,1)S(1)} %fusion.66, bf16[128,16,64]{0,2,1:T(8,128)(2,1)} %bitcast.121, bf16[768,16,64]{0,2,1:T(8,128)(2,1)} %bitcast.119), kind=kOutput, calls=%fused_computation.97.clone.1 | convolution fusion | flops 207618816 | bytes 8135424 | tf_op jit(solution)/shard_map/while/body/eval_jaxpr/sub | solution.py:60
  523.4 5.3 fusion.68
  528.7 1.1 copy.36
  530.5 4.0 convolution_convert_fusion.1
  535.4 4.1 fusion.24
  539.5 61.7 %reduce-scatter.2.cloned.1.call-done = bf16[128,1024]{1,0:T(8,128)(2,1)} async-done(((bf16[1024,1024]{1,0:T(8,128)(2,1)}), bf16[128,1024]{1,0:T(8,128)(2,1)}) %reduce-scatter.2.cloned.1.call-update) | async-done | bytes 262160 | tf_op jit(solution)/shard_map/reduce_scatter | solution.py:128
  601.2 1.1 fusion.32
  602.3 2.1 conditional.4
  602.4 1.9 collective-permute-done
  (97 shorter events, 18.2 us)
Async XLA Ops:
  7.2 523.4 %copy-start = (bf16[1,512,1024]{2,1,0:T(8,128)(2,1)S(1)}, bf16[1,512,1024]{2,1,0:T(8,128)(2,1)}, u32[]{:S(2)}) copy-start(bf16[1,512,1024]{2,1,0:T(8,128)(2,1)} %param.13) | copy-start | bytes 3145732
  7.2 86.7 %copy-start.3 = (bf16[1,128,3072]{2,1,0:T(8,128)(2,1)S(1)}, bf16[1,128,3072]{2,1,0:T(8,128)(2,1)}, u32[]{:S(2)}) copy-start(bf16[1,128,3072]{2,1,0:T(8,128)(2,1)} %param.14) | copy-start | bytes 2359300
  7.2 23.8 %collective-permute-start.2 = (bf16[128,3072]{1,0:T(8,128)(2,1)}, bf16[128,3072]{1,0:T(8,128)(2,1)S(1)}, u32[]{:S(2)}, u32[]{:S(2)}) collective-permute-start(bf16[128,3072]{1,0:T(8,128)(2,1)} %bitcast.124), channel_id=1, source_target_pairs={{0,1},{1,2},{2,3},{3,4},{4,5},{5,6},{6,7},{7,0},{8,9},{9,10},{10,1... | collective-permute-start | bytes 2359304 | tf_op jit(solution)/shard_map/ppermute | solution.py:23
  31.0 21.4 %collective-permute-start.3 = (bf16[128,3072]{1,0:T(8,128)(2,1)S(1)}, bf16[128,3072]{1,0:T(8,128)(2,1)S(1)}, u32[]{:S(2)}, u32[]{:S(2)}) collective-permute-start(bf16[128,3072]{1,0:T(8,128)(2,1)S(1)} %collective-permute-done.2), channel_id=1, source_target_pairs={{0,1},{1,2},{2,3},{3,4},{4,5},{5,6},{6,7},{7,0},{8,9},{9,10},{10,1... | collective-permute-start | bytes 2359304 | tf_op jit(solution)/shard_map/ppermute | solution.py:23
  52.4 20.7 %collective-permute-start.4 = (bf16[128,3072]{1,0:T(8,128)(2,1)S(1)}, bf16[128,3072]{1,0:T(8,128)(2,1)}, u32[]{:S(2)}, u32[]{:S(2)}) collective-permute-start(bf16[128,3072]{1,0:T(8,128)(2,1)S(1)} %collective-permute-done.3), channel_id=1, source_target_pairs={{0,1},{1,2},{2,3},{3,4},{4,5},{5,6},{6,7},{7,0},{8,9},{9,10},{10,1... | collective-permute-start | bytes 2359304 | tf_op jit(solution)/shard_map/ppermute | solution.py:23
  73.1 20.0 %collective-permute-start.5 = (bf16[128,3072]{1,0:T(8,128)(2,1)}, bf16[128,3072]{1,0:T(8,128)(2,1)}, u32[]{:S(2)}, u32[]{:S(2)}) collective-permute-start(bf16[128,3072]{1,0:T(8,128)(2,1)} %collective-permute-done.4), channel_id=1, source_target_pairs={{0,1},{1,2},{2,3},{3,4},{4,5},{5,6},{6,7},{7,0},{8,9},{9,10},{10,1... | collective-permute-start | bytes 2359304 | tf_op jit(solution)/shard_map/ppermute | solution.py:23
  93.1 19.0 %collective-permute-start.6 = (bf16[128,3072]{1,0:T(8,128)(2,1)}, bf16[128,3072]{1,0:T(8,128)(2,1)S(1)}, u32[]{:S(2)}, u32[]{:S(2)}) collective-permute-start(bf16[128,3072]{1,0:T(8,128)(2,1)} %collective-permute-done.5), channel_id=1, source_target_pairs={{0,1},{1,2},{2,3},{3,4},{4,5},{5,6},{6,7},{7,0},{8,9},{9,10},{10,1... | collective-permute-start | bytes 2359304 | tf_op jit(solution)/shard_map/ppermute | solution.py:23
  93.9 53.4 %copy-start.5 = (bf16[1,512,1024]{2,1,0:T(8,128)(2,1)S(1)}, bf16[1,512,1024]{2,1,0:T(8,128)(2,1)}, u32[]{:S(2)}) copy-start(bf16[1,512,1024]{2,1,0:T(8,128)(2,1)} %param.12) | copy-start | bytes 3145732
  112.1 18.0 %collective-permute-start.7 = (bf16[128,3072]{1,0:T(8,128)(2,1)S(1)}, bf16[128,3072]{1,0:T(8,128)(2,1)S(1)}, u32[]{:S(2)}, u32[]{:S(2)}) collective-permute-start(bf16[128,3072]{1,0:T(8,128)(2,1)S(1)} %collective-permute-done.6), channel_id=1, source_target_pairs={{0,1},{1,2},{2,3},{3,4},{4,5},{5,6},{6,7},{7,0},{8,9},{9,10},{10,1... | collective-permute-start | bytes 2359304 | tf_op jit(solution)/shard_map/ppermute | solution.py:23
  130.1 17.1 %collective-permute-start.8 = (bf16[128,3072]{1,0:T(8,128)(2,1)S(1)}, bf16[128,3072]{1,0:T(8,128)(2,1)S(1)}, u32[]{:S(2)}, u32[]{:S(2)}) collective-permute-start(bf16[128,3072]{1,0:T(8,128)(2,1)S(1)} %collective-permute-done.7), channel_id=1, source_target_pairs={{0,1},{1,2},{2,3},{3,4},{4,5},{5,6},{6,7},{7,0},{8,9},{9,10},{10,1... | collective-permute-start | bytes 2359304 | tf_op jit(solution)/shard_map/ppermute | solution.py:23
  151.0 1.6 copy-start.1
  164.7 6.4 %copy-start.7 = (s32[1,32]{1,0:T(1,128)S(1)}, s32[1,32]{1,0:T(1,128)}, u32[]{:S(2)}) copy-start(s32[1,32]{1,0:T(1,128)} %param.18) | copy-start | bytes 388
  164.7 208.1 %all-to-all-start = ((bf16[8,2,128,2048]{3,2,1,0:T(8,128)(2,1)}), bf16[8,2,128,2048]{3,2,1,0:T(8,128)(2,1)}, u32[]{:S(2)}, u32[]{:S(2)}) async-start(bf16[8,2,128,2048]{3,2,1,0:T(8,128)(2,1)} %broadcast_select_fusion.1), calls=%async_computation | async-start | bytes 16777216 | tf_op jit(solution)/shard_map/all_to_all | solution.py:112
  169.8 365.6 %all-gather.3.cloned.1.call-start = ((), (), s32[]{:S(2)}) async-start(), calls=%async_computation.3 | async-start | bytes 2359296 | tf_op jit(solution)/shard_map/all_gather | solution.py:126
  170.5 430.6 %reduce-scatter.2.cloned.1.call-start = ((), (), s32[]{:S(2)}) async-start(), calls=%async_computation.2 | async-start | bytes 2359296 | tf_op jit(solution)/shard_map/reduce_scatter | solution.py:128
  530.5 4.8 copy-start.6
  534.5 66.6 %copy-start.2 = (bf16[1,128,1024]{2,1,0:T(8,128)(2,1)S(1)}, bf16[1,128,1024]{2,1,0:T(8,128)(2,1)}, u32[]{:S(2)}) copy-start(bf16[1,128,1024]{2,1,0:T(8,128)(2,1)} %param.15) | copy-start | bytes 786436
  534.5 66.6 %copy-start.4 = (f32[1,128,1024]{2,1,0:T(8,128)S(1)}, f32[1,128,1024]{2,1,0:T(8,128)}, u32[]{:S(2)}) copy-start(f32[1,128,1024]{2,1,0:T(8,128)} %param.16) | copy-start | bytes 1572868
  602.3 2.0 collective-permute-start
Sparse Core Ops, SparseCore 0:
  172.7 164.8 all-gather.2
  534.6 66.4 reduce-scatter.1
